TPU v7x, 128 devices: a whole 4x4x4 slice. The times are simulated.
128 devices in a mesh: tok: 16 (over x, z), row: 4 (over y), col: 2 (over core).
Axes of the slice: x: 4, y: 4, z: 4, core: 2. Of those that a mesh axis runs over, the one named last changes fastest.
Arguments:
- block_input_rows: bfloat16 [8192, 4096], P(('tok', 'row'), 'col'), may hold values from -18 to 18
- input_norm_scale: bfloat16 [4096], P('col'), may hold values from 0.6 to 10, as said below
- query_key_value_weight: bfloat16 [4096, 16, 3, 128], P('col', 'row'), may hold values from -0.09375 to 0.09375
- adapter_down_weight: bfloat16 [4096, 128], P('col'), may hold values from -0.09375 to 0.09375
- adapter_up_weight: bfloat16 [128, 16, 3, 128], P(None, 'row'), may hold values from -0.5 to 0.5
- output_projection_weight: bfloat16 [2048, 2048], P(('row', 'col')), may hold values from -0.125 to 0.125
- prompt_segment_index: int32 [8192], replicated, may hold values from 0 to 3, never falling along the last dimension, each value on 1 to 4352 neighbouring positions
- cache_owner_index: int32 [8192, 1], P('tok'), may hold values from 0 to 15; in each aligned block of 512 rows (0 to 511, 512 to 1023, ...) at most 64 rows name the same one
Outputs:
- block_output: bfloat16 [8192, 2048], P(('tok', 'row', 'col'))
- kv_cache: bfloat16 [16384, 16, 2, 128], P('tok', ('row', 'col'))
Inputs may be any that keep to these rules, and one draw needn't show every extreme that they name: `prompt_segment_index`: never falls along the tokens; every prompt holds 1 to 4352 tokens and one holds exactly 4352. `cache_owner_index`: in each aligned block of 512 tokens no owner is named by more than 64 tokens; some owner is named exactly 64 times in some block. `input_norm_scale`: positive gains.
All inputs are finite; a program needn't handle non-finite values.
Results may differ from a plain program's by a relative error of at most 0.015.
The roundings to bfloat16 on the way count: a program that leaves them out, or rounds other values in their place, can miss the bound.
Values may be sent and summed in bfloat16 or wider, within the bound.
No kernel may reach another device: no remote copies, remote signals or barrier semaphores. Data moves between devices by JAX's collectives and lax.ppermute only.
A program may use at most 192 MiB of HBM per device.

v0:
```python
import jax
import jax.numpy as jnp
from jax import lax
from jax.sharding import PartitionSpec as P

INPUT_WIDTH = 4096
HEAD_SIZE = 128
ADAPTER_RANK = 128


def fold_piece(carry, piece, query, own_seg, own_start, prompt_segment_index, scale):
    top_old, total_old, acc_old = carry
    count = piece.shape[0]
    key_pos = jnp.arange(count, dtype=jnp.int32)
    query_pos = own_start + jnp.arange(query.shape[1], dtype=jnp.int32)
    allowed = (
        (own_seg[:, None] == prompt_segment_index[None, :])
        & (key_pos[None, :] <= query_pos[:, None])
        & (key_pos[None, :] >= 0)
    )
    score = (
        jnp.einsum("htd,shd->hts", query, piece[:, :, 0], preferred_element_type=jnp.float32)
        * scale
    )
    masked = jnp.where(allowed[None], score, -1e30)
    top_new = jnp.maximum(top_old, jnp.max(masked, axis=2))
    weights = jnp.where(allowed[None], jnp.exp(score - top_new[:, :, None]), 0.0).astype(
        jnp.bfloat16
    )
    total_new = jnp.sum(weights.astype(jnp.float32), axis=2)
    acc_new = jnp.einsum(
        "hts,shd->htd", weights, piece[:, :, 1], preferred_element_type=jnp.float32
    )
    return (top_new, total_new, acc_new)


def shards(
    block_input_rows,
    input_norm_scale,
    query_key_value_weight,
    adapter_down_weight,
    adapter_up_weight,
    output_projection_weight,
    prompt_segment_index,
    cache_owner_index,
):
    gathered = lax.all_gather(block_input_rows, "row", axis=0, tiled=True)
    wide = gathered.astype(jnp.float32)
    partial_sq = jnp.sum(wide * wide, axis=1)
    total_sq = lax.psum(partial_sq, "col")
    inverse = lax.rsqrt(total_sq / INPUT_WIDTH + 1e-06)
    normalized_input = (
        wide * inverse[:, None] * input_norm_scale.astype(jnp.float32)[None, :]
    ).astype(jnp.bfloat16)
    adapter_hidden = jnp.dot(
        normalized_input, adapter_down_weight, preferred_element_type=jnp.float32
    )
    tok_dev = gathered.shape[0]
    local_head_count = query_key_value_weight.shape[1]
    flat_weight = query_key_value_weight.reshape(
        query_key_value_weight.shape[0], local_head_count, 3 * HEAD_SIZE
    )
    flattened_up_weight = adapter_up_weight.reshape(ADAPTER_RANK, local_head_count, 3 * HEAD_SIZE)
    heads_dev = local_head_count // lax.axis_size("col")
    main = jnp.einsum(
        "td,dhe->hte", normalized_input, flat_weight, preferred_element_type=jnp.float32
    )
    adapter_down_output = jnp.einsum(
        "tr,rhe->hte",
        adapter_hidden,
        flattened_up_weight.astype(jnp.float32),
        precision=lax.Precision.HIGHEST,
    )
    mixed = lax.psum_scatter(main + adapter_down_output, "col", scatter_dimension=0, tiled=True)
    qkv = mixed.astype(jnp.bfloat16).reshape(heads_dev, tok_dev, 3, HEAD_SIZE)
    query = qkv[:, :, 0]
    kv_tok = jnp.transpose(qkv[:, :, 1:3], (1, 0, 2, 3))
    own_start = lax.axis_index("tok") * tok_dev
    own_seg = lax.dynamic_slice_in_dim(prompt_segment_index, own_start, tok_dev, 0)
    scale = 1.0 / HEAD_SIZE**0.5
    init = (
        jnp.full((heads_dev, tok_dev), -1e30, jnp.float32),
        jnp.zeros((heads_dev, tok_dev), jnp.float32),
        jnp.zeros((heads_dev, tok_dev, HEAD_SIZE), jnp.float32),
    )
    state = fold_piece(
        init,
        lax.all_gather(kv_tok, "tok", axis=0, tiled=True),
        query,
        own_seg,
        own_start,
        prompt_segment_index,
        scale,
    )
    attended = (state[2] / state[1][:, :, None]).astype(jnp.bfloat16)
    attended = jnp.transpose(attended, (1, 0, 2)).reshape(tok_dev, heads_dev * HEAD_SIZE)
    block_output = lax.psum_scatter(
        jnp.dot(attended, output_projection_weight, preferred_element_type=jnp.float32).astype(
            jnp.bfloat16
        ),
        ("row", "col"),
        scatter_dimension=0,
        tiled=True,
    )
    count_tok = lax.axis_size("tok")
    capacity = max(2, 2 * tok_dev // count_tok)
    owner = cache_owner_index[:, 0]
    onehot = (owner[:, None] == jnp.arange(count_tok, dtype=jnp.int32)[None, :]).astype(jnp.int32)
    before = jnp.cumsum(onehot, axis=0) - onehot
    rank = jnp.sum(before * onehot, axis=1)
    slot = owner * capacity + rank
    selector = (jnp.arange(count_tok * capacity, dtype=jnp.int32)[:, None] == slot[None, :]).astype(
        jnp.bfloat16
    )
    outgoing = jnp.dot(
        selector,
        kv_tok.reshape(tok_dev, heads_dev * 2 * HEAD_SIZE),
        preferred_element_type=jnp.float32,
    ).astype(jnp.bfloat16)
    received = lax.all_to_all(outgoing, "tok", split_axis=0, concat_axis=0, tiled=True)
    kv_cache = received.reshape(count_tok * capacity, heads_dev, 2, HEAD_SIZE)
    return (block_output, kv_cache)


def solution(mesh):
    placed = (
        P(("tok", "row"), "col"),
        P("col"),
        P("col", "row", None, None),
        P("col", None),
        P(None, "row", None, None),
        P(("row", "col"), None),
        P(),
        P("tok", None),
    )
    return jax.shard_map(
        shards,
        mesh=mesh,
        in_specs=placed,
        out_specs=(P(("tok", "row", "col"), None), P("tok", ("row", "col"), None, None)),
        check_vma=False,
    )
```

profile of v0, /device:TPU:0, one launch (start us, length us, event | category | flops | bytes accessed | tf_op | source)
XLA Modules:
  0.0 240.3 jit_solution(15088219014091748765)
XLA Ops:
  7.2 0.0 all-gather.3.cloned.1.call-start
  7.2 0.7 all-gather.3.cloned.1.call-update
  7.9 0.0 reduce-scatter.3.cloned.1.call-start
  8.0 0.7 convert_element_type.38
  8.7 10.7 %copy.13 = bf16[2048,4,3,128]{0,3,2,1:T(8,128)(2,1)} copy(bf16[2048,4,3,128]{3,1,2,0:T(4,128)(2,1)} %param.10) | data formatting | bytes 12582912 | tf_op args[2]
  19.4 0.3 copy.15
  19.7 23.3 %all-gather.3.cloned.1.call-done = bf16[512,2048]{1,0:T(8,128)(2,1)} async-done(((bf16[128,2048]{1,0:T(8,128)(2,1)}), bf16[512,2048]{1,0:T(8,128)(2,1)}) %all-gather.3.cloned.1.call-update) | async-done | bytes 2097168 | tf_op jit(solution)/shard_map/all_gather | solution.py:47
  43.0 2.1 fusion.1
  45.0 2.5 %psum.7 = f32[512]{0:T(512)S(1)} all-reduce(f32[512]{0:T(512)S(1)} %fusion.1), channel_id=1, replica_groups=mesh['tok'=16,'row'=4,'col'=2] {'col'}, use_global_device_ids=true, to_apply=%region_1.0 | all-reduce | flops 512 | bytes 4096 | tf_op jit(solution)/shard_map/psum | solution.py:50
  47.5 6.4 %fusion.6 = f32[512,4,384]{2,0,1:T(8,128)S(1)} fusion(bf16[2048,4,384]{0,2,1:T(8,128)(2,1)} %bitcast.71, bf16[512,2048]{1,0:T(8,128)(2,1)} %all-gather.3.cloned.1.call-done, f32[2048]{0:T(1024)S(1)} %convert_element_type.38, f32[512]{0:T(512)S(1)} %add_rsqrt_fusion), kind=kOutput, calls=%fused_computation.16 | convolution fusion | flops 3225419776 | bytes 11544576 | tf_op jit(solution)/shard_map/td,dhe->hte/dot_general | solution.py:65
  53.9 0.8 convolution_bitcast_fusion
  54.7 3.2 %add_bitcast_fusion = f32[4,512,384]{2,1,0:T(8,128)} fusion(f32[512,4,384]{2,0,1:T(8,128)S(1)} %fusion.6, f32[512,128,1]{1,0,2:T(8,128)S(1)} %convolution_bitcast_fusion, bf16[128,4,384]{0,2,1:T(8,128)(2,1)S(1)} %bitcast.76), kind=kOutput, calls=%fused_computation.14 | convolution fusion | flops 1208745984 | bytes 6946816 | tf_op jit(solution)/shard_map/tr,rhe->hte/dot_general | solution.py:68
  57.9 0.0 all-gather.5.cloned.1.call-start
  58.0 14.1 %reduce-scatter.3.cloned.1.call-done = f32[2,512,384]{2,1,0:T(8,128)} async-done(((f32[4,512,384]{2,1,0:T(8,128)}), f32[2,512,384]{2,1,0:T(8,128)}) %reduce-scatter.3.cloned.1.call-update) | async-done | bytes 1572880 | tf_op jit(solution)/shard_map/reduce_scatter | solution.py:74
  72.0 1.5 convert_element_type.40
  73.5 0.3 copy.17
  73.9 1.0 copy.27
  74.9 0.2 reduce-scatter.5.cloned.1.call-start
  75.1 0.1 dynamic_slice.3
  75.2 4.8 %fusion = pred[512,8192]{1,0:T(8,128)(4,1)} fusion(s32[512]{0:T(512)S(1)} %iota_add_fusion, s32[8192]{0:T(1024)S(1)} %copy-done.4, s32[512]{0:T(512)S(1)} %dynamic_slice.3), kind=kLoop, calls=%fused_computation.4 | loop fusion | flops 12582912 | bytes 4231168 | tf_op jit(solution)/shard_map/and | solution.py:17
  80.1 67.3 %all-gather.5.cloned.1.call-done = bf16[8192,2,2,128]{3,0,1,2:T(8,128)(2,1)} async-done(((bf16[512,2,2,128]{3,0,1,2:T(8,128)(2,1)}), bf16[8192,2,2,128]{3,0,1,2:T(8,128)(2,1)}) %all-gather.5.cloned.1.call-update) | async-done | bytes 8388624 | tf_op jit(solution)/shard_map/all_gather | solution.py:88
  147.4 17.6 %select_reduce_fusion = (f32[2,512]{1,0:T(2,128)S(1)}, f32[2,512,8192]{2,1,0:T(8,128)}) fusion(pred[512,8192]{1,0:T(8,128)(4,1)} %fusion, bf16[8192,2,2,128]{3,0,1,2:T(8,128)(2,1)} %all-gather.5.cloned.1.call-done, bf16[2,512,3,128]{1,3,2,0:T(8,128)(2,1)S(1)} %bitcast.73), kind=kOutput, calls=%fused_computation.2 | convolution fusion | flops 2172648448 | bytes 42209280 | tf_op jit(solution)/shard_map/htd,shd->hts/dot_general | solution.py:22
  164.9 16.2 %convert_reduce_fusion = f32[2,512]{1,0:T(2,128)S(1)} fusion(f32[2,512]{1,0:T(2,128)S(1)} %broadcast_maximum_fusion, f32[2,512,8192]{2,1,0:T(8,128)} %get-tuple-element.3, pred[512,8192]{1,0:T(8,128)(4,1)} %fusion), kind=kLoop, calls=%fused_computation | loop fusion | flops 50330624 | bytes 37756928 | tf_op jit(solution)/shard_map/reduce_sum | solution.py:30
  181.1 16.5 %fusion.12 = bf16[512,2,128]{0,2,1:T(8,128)(2,1)S(1)} fusion(bf16[8192,2,2,128]{3,0,1,2:T(8,128)(2,1)} %all-gather.5.cloned.1.call-done, f32[512,2]{0,1:T(2,128)S(1)} %bitcast.82, f32[2,512,8192]{2,1,0:T(8,128)} %get-tuple-element.3, f32[2,512]{1,0:T(2,128)S(1)} %broadcast_maximum_fusion, pred[512,8192]{1,0:T(8,128)(4,1)S(1)} %copy-done.1), kind=kOutput, calls=%fused_computation.23 | convolution fusion | flops 2181300224 | bytes 42213376 | tf_op jit(solution)/shard_map/hts,shd->htd/dot_general | solution.py:31
  197.7 2.1 convolution_convert_fusion
  199.8 1.2 reduce-window.6
  201.0 0.2 slice_reduce_fusion
  201.2 0.1 fusion.18
  201.3 0.7 fusion.9
  202.1 22.0 %all_to_all.9 = bf16[16,64,512]{2,1,0:T(8,128)(2,1)S(1)} all-to-all(bf16[16,64,512]{2,1,0:T(8,128)(2,1)S(1)} %bitcast.77), channel_id=1, replica_groups=mesh['tok'=16,'row'=4,'col'=2] {'tok'}, dimensions={0} | all-to-all | bytes 2097152 | tf_op jit(solution)/shard_map/all_to_all | solution.py:120
  224.1 1.1 reshape.115
  225.2 8.6 %reduce-scatter.5.cloned.1.call-done = bf16[64,2048]{1,0:T(8,128)(2,1)} async-done(((bf16[512,2048]{1,0:T(8,128)(2,1)}), bf16[64,2048]{1,0:T(8,128)(2,1)}) %reduce-scatter.5.cloned.1.call-update) | async-done | bytes 262160 | tf_op jit(solution)/shard_map/reduce_scatter | solution.py:97
  (25 shorter events, 0.2 us)
Async XLA Ops:
  7.2 190.5 %copy-start = (bf16[256,2048]{1,0:T(8,128)(2,1)S(1)}, bf16[256,2048]{1,0:T(8,128)(2,1)}, u32[]{:S(2)}) copy-start(bf16[256,2048]{1,0:T(8,128)(2,1)} %param.13) | copy-start | bytes 3145732
  7.2 35.8 %all-gather.3.cloned.1.call-start = ((), (), s32[]{:S(2)}) async-start(), calls=%async_computation.3 | async-start | bytes 2621440 | tf_op jit(solution)/shard_map/all_gather | solution.py:47
  7.9 64.1 %reduce-scatter.3.cloned.1.call-start = ((), (), s32[]{:S(2)}) async-start(), calls=%async_computation.4 | async-start | bytes 4718592 | tf_op jit(solution)/shard_map/reduce_scatter | solution.py:74
  8.7 10.7 %copy-start.3 = (bf16[128,4,3,128]{3,1,2,0:T(4,128)(2,1)S(1)}, bf16[128,4,3,128]{3,1,2,0:T(4,128)(2,1)}, u32[]{:S(2)}) copy-start(bf16[128,4,3,128]{3,1,2,0:T(4,128)(2,1)} %param.12) | copy-start | bytes 1179652
  47.5 6.4 %copy-start.2 = (bf16[512,2048]{1,0:T(8,128)(2,1)S(1)}, bf16[512,2048]{1,0:T(8,128)(2,1)}, u32[]{:S(2)}) copy-start(bf16[512,2048]{1,0:T(8,128)(2,1)} %all-gather.3.cloned.1.call-done) | copy-start | bytes 6291460
  47.5 6.4 %copy-start.6 = (bf16[2048,128]{1,0:T(8,128)(2,1)S(1)}, bf16[2048,128]{1,0:T(8,128)(2,1)}, u32[]{:S(2)}) copy-start(bf16[2048,128]{1,0:T(8,128)(2,1)} %param.11) | copy-start | bytes 1572868
  57.9 17.2 %copy-start.4 = (s32[8192]{0:T(1024)S(1)}, s32[8192]{0:T(1024)}, u32[]{:S(2)}) copy-start(s32[8192]{0:T(1024)} %param.14) | copy-start | bytes 98308
  57.9 89.4 %all-gather.5.cloned.1.call-start = ((), (), s32[]{:S(2)}) async-start(), calls=%async_computation.5 | async-start | bytes 8912896 | tf_op jit(solution)/shard_map/all_gather | solution.py:88
  74.9 158.9 %reduce-scatter.5.cloned.1.call-start = ((), (), s32[]{:S(2)}) async-start(), calls=%async_computation.6 | async-start | bytes 2359296 | tf_op jit(solution)/shard_map/reduce_scatter | solution.py:97
  164.9 16.2 %copy-start.1 = (pred[512,8192]{1,0:T(8,128)(4,1)S(1)}, pred[512,8192]{1,0:T(8,128)(4,1)}, u32[]{:S(2)}) copy-start(pred[512,8192]{1,0:T(8,128)(4,1)} %fusion) | copy-start | bytes 12582916
  197.6 2.1 copy-start.5
Sparse Core Ops, SparseCore 0:
  9.6 33.2 all-gather.2
  58.0 13.9 reduce-scatter.2
  75.0 72.3 all-gather.4
  199.9 33.8 reduce-scatter.4
where the time goes:
time: 241 us; the launch traced here: 240 us
  waiting for transfers between devices  114 us (47%)
  matrix products  47.2 us (20%)
  other arithmetic  26.6 us (11%)
  blocking collectives  24.5 us (10%)
  between operations  13.9 us (6%)
  local copies, waits for them, and re-layouts  13.8 us (6%)
    all_gather x1, waiting for transfers between devices, shards(): lax.all_gather(kv_tok, 'tok', axis=0, tiled=True)  67.3 us
    all_gather x1, waiting for transfers between devices, shards(): gathered = lax.all_gather(block_input_rows, 'row', axis=0, tiled=True)  23.3 us
    all_to_all x1, blocking collectives, shards(): lax.all_to_all(outgoing, 'tok', split_axis=0, concat_axis=0, tiled=True)  22 us
    dot_general x1, matrix products, fold_piece(): jnp.einsum('htd,shd->hts', query, piece[:, :, 0], preferred_element_type=...  17.6 us
    dot_general x1, matrix products, fold_piece(): jnp.einsum('hts,shd->htd', weights, piece[:, :, 1], preferred_element_typ...  16.5 us
    reduce_sum x1, other arithmetic, fold_piece(): total_new = jnp.sum(weights.astype(jnp.float32), axis=2)  16.2 us
    reduce_scatter x1, waiting for transfers between devices, shards(): lax.psum_scatter(main + adapter_down_output, 'col', scatter_dimension=0,...  14.1 us
    unnamed x17, local copies, waits for them, and re-layouts  12.1 us
  transfers between devices with their start and end apart: 4, of which 4 were waited for; matrix products, arithmetic and copies ran while one was open for 8% of the time, Pallas kernels for 0%

commit v1 on v0

--- a/solution.py
+++ b/solution.py
@@ -6,6 +6,29 @@
 INPUT_WIDTH = 4096
 HEAD_SIZE = 128
 ADAPTER_RANK = 128
+
+
+def cut_along(shard, dim, size):
+    shape = shard.shape
+    blocks = shard.reshape(*shape[:dim], size, shape[dim] // size, *shape[dim + 1 :])
+    return jnp.moveaxis(blocks, dim, 0)
+
+
+def in_order(pieces, dim):
+    pieces = jnp.moveaxis(pieces, 0, dim)
+    shape = pieces.shape
+    return pieces.reshape(*shape[:dim], shape[dim] * shape[dim + 1], *shape[dim + 2 :])
+
+
+def swapped_with_each(x, axis, split_dim, concat_dim):
+    devices, mine = (lax.axis_size(axis), lax.axis_index(axis))
+    blocks = cut_along(x, split_dim, devices)
+    outs = [blocks[mine]]
+    for step in range(1, devices):
+        sent = blocks[mine ^ step]
+        outs.append(lax.ppermute(sent, axis, [(i, i ^ step) for i in range(devices)]))
+    blocks = jnp.stack(outs)[mine ^ jnp.arange(devices)]
+    return in_order(blocks, concat_dim)
 
 
 def fold_piece(carry, piece, query, own_seg, own_start, prompt_segment_index, scale):
@@ -117,7 +140,7 @@
         kv_tok.reshape(tok_dev, heads_dev * 2 * HEAD_SIZE),
         preferred_element_type=jnp.float32,
     ).astype(jnp.bfloat16)
-    received = lax.all_to_all(outgoing, "tok", split_axis=0, concat_axis=0, tiled=True)
+    received = swapped_with_each(outgoing, "tok", 0, 0)
     kv_cache = received.reshape(count_tok * capacity, heads_dev, 2, HEAD_SIZE)
     return (block_output, kv_cache)
 

time: 241 us -> 247 us (1.025)
  starting transfers between devices: 0.34 us -> 32.4 us
  blocking collectives: 24.5 us -> 2.47 us
  waiting for transfers between devices: 114 us -> 110 us
    ppermute x0 -> x15, starting transfers between devices: none -> 32.1 us  [swapped_with_each(): lax.ppermute(sent, axis, [(i, i ^ step) for i in range(devices)])]
    all_to_all x1 -> x0, blocking collectives: 22 us -> none  [shards(): lax.all_to_all(outgoing, 'tok', split_axis=0, concat_axis=0, tiled=True)]
    reduce_scatter x1, waiting for transfers between devices: 8.58 us -> 0.01 us  [shards(): lax.psum_scatter(jnp.dot(attended, output_projection_weight, preferred_el...]
    ppermute x0 -> x15, waiting for transfers between devices: none -> 5.17 us  [swapped_with_each(): lax.ppermute(sent, axis, [(i, i ^ step) for i in range(devices)])]
    unnamed x17 -> x33, local copies, waits for them, and re-layouts: 12.1 us -> 12.1 us
  transfers between devices with their start and end apart: 4 -> 19, of which waited for: 4 -> 5; matrix products, arithmetic and copies ran while one was open for 8% -> 8% of each run, Pallas kernels for 0% -> 0%
where the time goes in v1:
time: 247 us
  waiting for transfers between devices  110 us (45%)
  matrix products  47.4 us (19%)
  starting transfers between devices  32.4 us (13%)
  other arithmetic  26 us (11%)
  local copies, waits for them, and re-layouts  14.6 us (6%)
  between operations  14.2 us (6%)
  blocking collectives  2.47 us (1%)
    all_gather x1, waiting for transfers between devices, shards(): lax.all_gather(kv_tok, 'tok', axis=0, tiled=True)  65.8 us
    ppermute x15, starting transfers between devices, swapped_with_each(): lax.ppermute(sent, axis, [(i, i ^ step) for i in range(devices)])  32.1 us
    all_gather x1, waiting for transfers between devices, shards(): gathered = lax.all_gather(block_input_rows, 'row', axis=0, tiled=True)  24 us
    dot_general x1, matrix products, fold_piece(): jnp.einsum('htd,shd->hts', query, piece[:, :, 0], preferred_element_type=...  17.6 us
    dot_general x1, matrix products, fold_piece(): jnp.einsum('hts,shd->htd', weights, piece[:, :, 1], preferred_element_typ...  16.7 us
    reduce_sum x1, other arithmetic, fold_piece(): total_new = jnp.sum(weights.astype(jnp.float32), axis=2)  16.2 us
    reduce_scatter x1, waiting for transfers between devices, shards(): lax.psum_scatter(main + adapter_down_output, 'col', scatter_dimension=0,...  14.1 us
    unnamed x33, local copies, waits for them, and re-layouts  12.1 us
  transfers between devices with their start and end apart: 19, of which 5 were waited for; matrix products, arithmetic and copies ran while one was open for 8% of the time, Pallas kernels for 0%

profile of v1, /device:TPU:0, one launch (start us, length us, event | category | flops | bytes accessed | tf_op | source)
XLA Modules:
  0.0 246.7 jit_solution(2513038588804557553)
XLA Ops:
  8.0 10.7 %copy.13 = bf16[2048,4,3,128]{0,3,2,1:T(8,128)(2,1)} copy(bf16[2048,4,3,128]{3,1,2,0:T(4,128)(2,1)} %param.10) | data formatting | bytes 12582912 | tf_op args[2]
  19.0 24.0 %all-gather.3.cloned.1.call-done = bf16[512,2048]{1,0:T(8,128)(2,1)} async-done(((bf16[128,2048]{1,0:T(8,128)(2,1)}), bf16[512,2048]{1,0:T(8,128)(2,1)}) %all-gather.3.cloned.1.call-update) | async-done | bytes 2097168 | tf_op jit(solution)/shard_map/all_gather | solution.py:70
  43.0 2.1 fusion.1
  45.0 2.5 psum.7
  47.5 6.4 %fusion.6 = f32[512,4,384]{2,0,1:T(8,128)S(1)} fusion(bf16[2048,4,384]{0,2,1:T(8,128)(2,1)} %bitcast.133, bf16[512,2048]{1,0:T(8,128)(2,1)} %all-gather.3.cloned.1.call-done, f32[2048]{0:T(1024)S(1)} %convert_element_type.38, f32[512]{0:T(512)S(1)} %add_rsqrt_fusion), kind=kOutput, calls=%fused_computation.17 | convolution fusion | flops 3225419776 | bytes 11544576 | tf_op jit(solution)/shard_map/td,dhe->hte/dot_general | solution.py:88
  54.0 0.8 convolution_bitcast_fusion
  54.7 3.1 %add_bitcast_fusion = f32[4,512,384]{2,1,0:T(8,128)} fusion(f32[512,4,384]{2,0,1:T(8,128)S(1)} %fusion.6, f32[512,128,1]{1,0,2:T(8,128)S(1)} %convolution_bitcast_fusion, bf16[128,4,384]{0,2,1:T(8,128)(2,1)S(1)} %bitcast.138), kind=kOutput, calls=%fused_computation.15 | convolution fusion | flops 1208745984 | bytes 6946816 | tf_op jit(solution)/shard_map/tr,rhe->hte/dot_general | solution.py:91
  58.0 14.1 %reduce-scatter.3.cloned.1.call-done = f32[2,512,384]{2,1,0:T(8,128)} async-done(((f32[4,512,384]{2,1,0:T(8,128)}), f32[2,512,384]{2,1,0:T(8,128)}) %reduce-scatter.3.cloned.1.call-update) | async-done | bytes 1572880 | tf_op jit(solution)/shard_map/reduce_scatter | solution.py:97
  72.0 1.5 convert_element_type.40
  73.8 1.0 copy.27
  75.1 1.2 reduce-window.6
  76.7 4.9 %fusion = pred[512,8192]{1,0:T(8,128)(4,1)} fusion(s32[512]{0:T(512)S(1)} %iota_add_fusion, s32[8192]{0:T(1024)S(1)} %copy-done.4, s32[512]{0:T(512)S(1)} %dynamic_slice.51), kind=kLoop, calls=%fused_computation.5 | loop fusion | flops 12582912 | bytes 4231168 | tf_op jit(solution)/shard_map/and | solution.py:40
  81.6 65.8 %all-gather.5.cloned.1.call-done = bf16[8192,2,2,128]{3,0,1,2:T(8,128)(2,1)} async-done(((bf16[512,2,2,128]{3,0,1,2:T(8,128)(2,1)}), bf16[8192,2,2,128]{3,0,1,2:T(8,128)(2,1)}) %all-gather.5.cloned.1.call-update) | async-done | bytes 8388624 | tf_op jit(solution)/shard_map/all_gather | solution.py:111
  147.3 17.6 %select_reduce_fusion = (f32[2,512]{1,0:T(2,128)S(1)}, f32[2,512,8192]{2,1,0:T(8,128)}) fusion(pred[512,8192]{1,0:T(8,128)(4,1)} %fusion, bf16[8192,2,2,128]{3,0,1,2:T(8,128)(2,1)} %all-gather.5.cloned.1.call-done, bf16[2,512,3,128]{1,3,2,0:T(8,128)(2,1)S(1)} %bitcast.135), kind=kOutput, calls=%fused_computation.3 | convolution fusion | flops 2172648448 | bytes 42209280 | tf_op jit(solution)/shard_map/htd,shd->hts/dot_general | solution.py:45
  164.9 16.2 %convert_reduce_fusion = f32[2,512]{1,0:T(2,128)S(1)} fusion(f32[2,512]{1,0:T(2,128)S(1)} %broadcast_maximum_fusion, f32[2,512,8192]{2,1,0:T(8,128)} %get-tuple-element.19, pred[512,8192]{1,0:T(8,128)(4,1)} %fusion), kind=kLoop, calls=%fused_computation.1 | loop fusion | flops 50330624 | bytes 37756928 | tf_op jit(solution)/shard_map/reduce_sum | solution.py:53
  181.1 16.7 %fusion.12 = bf16[512,2,128]{0,2,1:T(8,128)(2,1)S(1)} fusion(bf16[8192,2,2,128]{3,0,1,2:T(8,128)(2,1)} %all-gather.5.cloned.1.call-done, f32[512,2]{0,1:T(2,128)S(1)} %bitcast.144, f32[2,512,8192]{2,1,0:T(8,128)} %get-tuple-element.19, f32[2,512]{1,0:T(2,128)S(1)} %broadcast_maximum_fusion, pred[512,8192]{1,0:T(8,128)(4,1)S(1)} %copy-done.1), kind=kOutput, calls=%fused_computation.24 | convolution fusion | flops 2181300224 | bytes 42213376 | tf_op jit(solution)/shard_map/hts,shd->htd/dot_general | solution.py:54
  197.9 2.1 convolution_convert_fusion
  200.1 0.7 fusion.9
  201.0 1.4 collective-permute-start
  202.4 2.9 %collective-permute-start.1 = (bf16[64,512]{1,0:T(8,128)(2,1)S(1)}, bf16[64,512]{1,0:T(8,128)(2,1)S(1)}, u32[]{:S(2)}, u32[]{:S(2)}) collective-permute-start(bf16[64,512]{1,0:T(8,128)(2,1)S(1)} %get-tuple-element.15), channel_id=1, source_target_pairs={{0,16},{8,24},{16,0},{24,8},{32,48},{40,56},{48,32},{56,40},{64,80... | collective-permute-start | bytes 196616 | tf_op jit(solution)/shard_map/ppermute | solution.py:29
  205.8 1.5 collective-permute-start.3
  207.3 3.7 %collective-permute-start.5 = (bf16[64,512]{1,0:T(8,128)(2,1)S(1)}, bf16[64,512]{1,0:T(8,128)(2,1)S(1)}, u32[]{:S(2)}, u32[]{:S(2)}) collective-permute-start(bf16[64,512]{1,0:T(8,128)(2,1)S(1)} %get-tuple-element.11), channel_id=1, source_target_pairs={{0,48},{8,56},{16,32},{24,40},{32,16},{40,24},{48,0},{56,8},{64,11... | collective-permute-start | bytes 196616 | tf_op jit(solution)/shard_map/ppermute | solution.py:29
  211.1 1.8 collective-permute-start.6
  213.0 3.1 %collective-permute-start.7 = (bf16[64,512]{1,0:T(8,128)(2,1)S(1)}, bf16[64,512]{1,0:T(8,128)(2,1)S(1)}, u32[]{:S(2)}, u32[]{:S(2)}) collective-permute-start(bf16[64,512]{1,0:T(8,128)(2,1)S(1)} %get-tuple-element.9), channel_id=1, source_target_pairs={{0,64},{8,72},{16,80},{24,88},{32,96},{40,104},{48,112},{56,120},{... | collective-permute-start | bytes 196616 | tf_op jit(solution)/shard_map/ppermute | solution.py:29
  216.2 5.1 %collective-permute-start.9 = (bf16[64,512]{1,0:T(8,128)(2,1)S(1)}, bf16[64,512]{1,0:T(8,128)(2,1)S(1)}, u32[]{:S(2)}, u32[]{:S(2)}) collective-permute-start(bf16[64,512]{1,0:T(8,128)(2,1)S(1)} %get-tuple-element.7), channel_id=1, source_target_pairs={{0,80},{8,88},{16,64},{24,72},{32,112},{40,120},{48,96},{56,104},{... | collective-permute-start | bytes 196616 | tf_op jit(solution)/shard_map/ppermute | solution.py:29
  221.2 2.1 collective-permute-start.10
  223.4 2.8 %collective-permute-start.11 = (bf16[64,512]{1,0:T(8,128)(2,1)S(1)}, bf16[64,512]{1,0:T(8,128)(2,1)S(1)}, u32[]{:S(2)}, u32[]{:S(2)}) collective-permute-start(bf16[64,512]{1,0:T(8,128)(2,1)S(1)} %get-tuple-element.5), channel_id=1, source_target_pairs={{0,96},{8,104},{16,112},{24,120},{32,64},{40,72},{48,80},{56,88},{... | collective-permute-start | bytes 196616 | tf_op jit(solution)/shard_map/ppermute | solution.py:29
  226.3 4.5 %collective-permute-start.13 = (bf16[64,512]{1,0:T(8,128)(2,1)S(1)}, bf16[64,512]{1,0:T(8,128)(2,1)S(1)}, u32[]{:S(2)}, u32[]{:S(2)}) collective-permute-start(bf16[64,512]{1,0:T(8,128)(2,1)S(1)} %get-tuple-element.3), channel_id=1, source_target_pairs={{0,112},{8,120},{16,96},{24,104},{32,80},{40,88},{48,64},{56,72},{... | collective-permute-start | bytes 196616 | tf_op jit(solution)/shard_map/ppermute | solution.py:29
  230.8 2.4 collective-permute-start.14
  233.3 1.0 collective-permute-done.13
  234.3 4.2 %collective-permute-done.14 = bf16[64,512]{1,0:T(8,128)(2,1)S(1)} collective-permute-done((bf16[64,512]{1,0:T(8,128)(2,1)S(1)}, bf16[64,512]{1,0:T(8,128)(2,1)S(1)}, u32[]{:S(2)}, u32[]{:S(2)}) %collective-permute-start.14) | collective-permute-done | bytes 65568 | tf_op jit(solution)/shard_map/ppermute | solution.py:29
  239.1 1.1 reshape_reshape.3
  (75 shorter events, 3.9 us)
Async XLA Ops:
  7.2 190.7 %copy-start = (bf16[256,2048]{1,0:T(8,128)(2,1)S(1)}, bf16[256,2048]{1,0:T(8,128)(2,1)}, u32[]{:S(2)}) copy-start(bf16[256,2048]{1,0:T(8,128)(2,1)} %param.13) | copy-start | bytes 3145732
  7.2 35.8 %all-gather.3.cloned.1.call-start = ((), (), s32[]{:S(2)}) async-start(), calls=%async_computation.2 | async-start | bytes 2621440 | tf_op jit(solution)/shard_map/all_gather | solution.py:70
  7.9 10.8 %copy-start.6 = (bf16[2048]{0:T(1024)(128)(2,1)S(1)}, bf16[2048]{0:T(1024)(128)(2,1)}, u32[]{:S(2)}) copy-start(bf16[2048]{0:T(1024)(128)(2,1)} %param.9) | copy-start | bytes 12292
  7.9 10.7 %copy-start.3 = (bf16[128,4,3,128]{3,1,2,0:T(4,128)(2,1)S(1)}, bf16[128,4,3,128]{3,1,2,0:T(4,128)(2,1)}, u32[]{:S(2)}) copy-start(bf16[128,4,3,128]{3,1,2,0:T(4,128)(2,1)} %param.12) | copy-start | bytes 1179652
  7.9 64.1 %reduce-scatter.3.cloned.1.call-start = ((), (), s32[]{:S(2)}) async-start(), calls=%async_computation.3 | async-start | bytes 4718592 | tf_op jit(solution)/shard_map/reduce_scatter | solution.py:97
  47.5 6.4 %copy-start.2 = (bf16[512,2048]{1,0:T(8,128)(2,1)S(1)}, bf16[512,2048]{1,0:T(8,128)(2,1)}, u32[]{:S(2)}) copy-start(bf16[512,2048]{1,0:T(8,128)(2,1)} %all-gather.3.cloned.1.call-done) | copy-start | bytes 6291460
  47.5 6.4 %copy-start.7 = (bf16[2048,128]{1,0:T(8,128)(2,1)S(1)}, bf16[2048,128]{1,0:T(8,128)(2,1)}, u32[]{:S(2)}) copy-start(bf16[2048,128]{1,0:T(8,128)(2,1)} %param.11) | copy-start | bytes 1572868
  57.9 17.2 %copy-start.5 = (s32[512,1]{0,1:T(1,128)S(1)}, s32[512,1]{0,1:T(1,128)}, u32[]{:S(2)}) copy-start(s32[512,1]{0,1:T(1,128)} %param.15) | copy-start | bytes 6148
  57.9 18.7 %copy-start.4 = (s32[8192]{0:T(1024)S(1)}, s32[8192]{0:T(1024)}, u32[]{:S(2)}) copy-start(s32[8192]{0:T(1024)} %param.14) | copy-start | bytes 98308
  57.9 89.4 %all-gather.5.cloned.1.call-start = ((), (), s32[]{:S(2)}) async-start(), calls=%async_computation.4 | async-start | bytes 8912896 | tf_op jit(solution)/shard_map/all_gather | solution.py:111
  74.9 165.3 %reduce-scatter.5.cloned.1.call-start = ((), (), s32[]{:S(2)}) async-start(), calls=%async_computation.5 | async-start | bytes 2359296 | tf_op jit(solution)/shard_map/reduce_scatter | solution.py:120
  164.9 16.2 %copy-start.1 = (pred[512,8192]{1,0:T(8,128)(4,1)S(1)}, pred[512,8192]{1,0:T(8,128)(4,1)}, u32[]{:S(2)}) copy-start(pred[512,8192]{1,0:T(8,128)(4,1)} %fusion) | copy-start | bytes 12582916
  201.0 6.3 %collective-permute-start = (bf16[64,512]{1,0:T(8,128)(2,1)S(1)}, bf16[64,512]{1,0:T(8,128)(2,1)S(1)}, u32[]{:S(2)}, u32[]{:S(2)}) collective-permute-start(bf16[64,512]{1,0:T(8,128)(2,1)S(1)} %get-tuple-element.16), channel_id=1, source_target_pairs={{0,8},{8,0},{16,24},{24,16},{32,40},{40,32},{48,56},{56,48},{64,72... | collective-permute-start | bytes 196616 | tf_op jit(solution)/shard_map/ppermute | solution.py:29
  202.4 8.7 %collective-permute-start.1 = (bf16[64,512]{1,0:T(8,128)(2,1)S(1)}, bf16[64,512]{1,0:T(8,128)(2,1)S(1)}, u32[]{:S(2)}, u32[]{:S(2)}) collective-permute-start(bf16[64,512]{1,0:T(8,128)(2,1)S(1)} %get-tuple-element.15), channel_id=1, source_target_pairs={{0,16},{8,24},{16,0},{24,8},{32,48},{40,56},{48,32},{56,40},{64,80... | collective-permute-start | bytes 196616 | tf_op jit(solution)/shard_map/ppermute | solution.py:29
  205.2 7.7 %collective-permute-start.2 = (bf16[64,512]{1,0:T(8,128)(2,1)S(1)}, bf16[64,512]{1,0:T(8,128)(2,1)S(1)}, u32[]{:S(2)}, u32[]{:S(2)}) collective-permute-start(bf16[64,512]{1,0:T(8,128)(2,1)S(1)} %get-tuple-element.14), channel_id=1, source_target_pairs={{0,24},{8,16},{16,8},{24,0},{32,56},{40,48},{48,40},{56,32},{64,88... | collective-permute-start | bytes 196616 | tf_op jit(solution)/shard_map/ppermute | solution.py:29
  205.8 10.2 %collective-permute-start.3 = (bf16[64,512]{1,0:T(8,128)(2,1)S(1)}, bf16[64,512]{1,0:T(8,128)(2,1)S(1)}, u32[]{:S(2)}, u32[]{:S(2)}) collective-permute-start(bf16[64,512]{1,0:T(8,128)(2,1)S(1)} %get-tuple-element.13), channel_id=1, source_target_pairs={{0,32},{8,40},{16,48},{24,56},{32,0},{40,8},{48,16},{56,24},{64,96... | collective-permute-start | bytes 196616 | tf_op jit(solution)/shard_map/ppermute | solution.py:29
  207.3 8.9 %collective-permute-start.4 = (bf16[64,512]{1,0:T(8,128)(2,1)S(1)}, bf16[64,512]{1,0:T(8,128)(2,1)S(1)}, u32[]{:S(2)}, u32[]{:S(2)}) collective-permute-start(bf16[64,512]{1,0:T(8,128)(2,1)S(1)} %get-tuple-element.12), channel_id=1, source_target_pairs={{0,40},{8,32},{16,56},{24,48},{32,8},{40,0},{48,24},{56,16},{64,10... | collective-permute-start | bytes 196616 | tf_op jit(solution)/shard_map/ppermute | solution.py:29
  207.3 13.9 %collective-permute-start.5 = (bf16[64,512]{1,0:T(8,128)(2,1)S(1)}, bf16[64,512]{1,0:T(8,128)(2,1)S(1)}, u32[]{:S(2)}, u32[]{:S(2)}) collective-permute-start(bf16[64,512]{1,0:T(8,128)(2,1)S(1)} %get-tuple-element.11), channel_id=1, source_target_pairs={{0,48},{8,56},{16,32},{24,40},{32,16},{40,24},{48,0},{56,8},{64,11... | collective-permute-start | bytes 196616 | tf_op jit(solution)/shard_map/ppermute | solution.py:29
  211.1 12.3 %collective-permute-start.6 = (bf16[64,512]{1,0:T(8,128)(2,1)S(1)}, bf16[64,512]{1,0:T(8,128)(2,1)S(1)}, u32[]{:S(2)}, u32[]{:S(2)}) collective-permute-start(bf16[64,512]{1,0:T(8,128)(2,1)S(1)} %get-tuple-element.10), channel_id=1, source_target_pairs={{0,56},{8,48},{16,40},{24,32},{32,24},{40,16},{48,8},{56,0},{64,12... | collective-permute-start | bytes 196616 | tf_op jit(solution)/shard_map/ppermute | solution.py:29
  213.0 13.2 %collective-permute-start.7 = (bf16[64,512]{1,0:T(8,128)(2,1)S(1)}, bf16[64,512]{1,0:T(8,128)(2,1)S(1)}, u32[]{:S(2)}, u32[]{:S(2)}) collective-permute-start(bf16[64,512]{1,0:T(8,128)(2,1)S(1)} %get-tuple-element.9), channel_id=1, source_target_pairs={{0,64},{8,72},{16,80},{24,88},{32,96},{40,104},{48,112},{56,120},{... | collective-permute-start | bytes 196616 | tf_op jit(solution)/shard_map/ppermute | solution.py:29
  216.0 10.3 %collective-permute-start.8 = (bf16[64,512]{1,0:T(8,128)(2,1)S(1)}, bf16[64,512]{1,0:T(8,128)(2,1)S(1)}, u32[]{:S(2)}, u32[]{:S(2)}) collective-permute-start(bf16[64,512]{1,0:T(8,128)(2,1)S(1)} %get-tuple-element.8), channel_id=1, source_target_pairs={{0,72},{8,64},{16,88},{24,80},{32,104},{40,96},{48,120},{56,112},{... | collective-permute-start | bytes 196616 | tf_op jit(solution)/shard_map/ppermute | solution.py:29
  216.2 14.6 %collective-permute-start.9 = (bf16[64,512]{1,0:T(8,128)(2,1)S(1)}, bf16[64,512]{1,0:T(8,128)(2,1)S(1)}, u32[]{:S(2)}, u32[]{:S(2)}) collective-permute-start(bf16[64,512]{1,0:T(8,128)(2,1)S(1)} %get-tuple-element.7), channel_id=1, source_target_pairs={{0,80},{8,88},{16,64},{24,72},{32,112},{40,120},{48,96},{56,104},{... | collective-permute-start | bytes 196616 | tf_op jit(solution)/shard_map/ppermute | solution.py:29
  221.2 12.0 %collective-permute-start.10 = (bf16[64,512]{1,0:T(8,128)(2,1)S(1)}, bf16[64,512]{1,0:T(8,128)(2,1)S(1)}, u32[]{:S(2)}, u32[]{:S(2)}) collective-permute-start(bf16[64,512]{1,0:T(8,128)(2,1)S(1)} %get-tuple-element.6), channel_id=1, source_target_pairs={{0,88},{8,80},{16,72},{24,64},{32,120},{40,112},{48,104},{56,96},{... | collective-permute-start | bytes 196616 | tf_op jit(solution)/shard_map/ppermute | solution.py:29
  223.4 9.9 %collective-permute-start.11 = (bf16[64,512]{1,0:T(8,128)(2,1)S(1)}, bf16[64,512]{1,0:T(8,128)(2,1)S(1)}, u32[]{:S(2)}, u32[]{:S(2)}) collective-permute-start(bf16[64,512]{1,0:T(8,128)(2,1)S(1)} %get-tuple-element.5), channel_id=1, source_target_pairs={{0,96},{8,104},{16,112},{24,120},{32,64},{40,72},{48,80},{56,88},{... | collective-permute-start | bytes 196616 | tf_op jit(solution)/shard_map/ppermute | solution.py:29
  226.2 7.1 %collective-permute-start.12 = (bf16[64,512]{1,0:T(8,128)(2,1)S(1)}, bf16[64,512]{1,0:T(8,128)(2,1)S(1)}, u32[]{:S(2)}, u32[]{:S(2)}) collective-permute-start(bf16[64,512]{1,0:T(8,128)(2,1)S(1)} %get-tuple-element.4), channel_id=1, source_target_pairs={{0,104},{8,96},{16,120},{24,112},{32,72},{40,64},{48,88},{56,80},{... | collective-permute-start | bytes 196616 | tf_op jit(solution)/shard_map/ppermute | solution.py:29
  226.3 8.0 %collective-permute-start.13 = (bf16[64,512]{1,0:T(8,128)(2,1)S(1)}, bf16[64,512]{1,0:T(8,128)(2,1)S(1)}, u32[]{:S(2)}, u32[]{:S(2)}) collective-permute-start(bf16[64,512]{1,0:T(8,128)(2,1)S(1)} %get-tuple-element.3), channel_id=1, source_target_pairs={{0,112},{8,120},{16,96},{24,104},{32,80},{40,88},{48,64},{56,72},{... | collective-permute-start | bytes 196616 | tf_op jit(solution)/shard_map/ppermute | solution.py:29
  230.8 7.7 %collective-permute-start.14 = (bf16[64,512]{1,0:T(8,128)(2,1)S(1)}, bf16[64,512]{1,0:T(8,128)(2,1)S(1)}, u32[]{:S(2)}, u32[]{:S(2)}) collective-permute-start(bf16[64,512]{1,0:T(8,128)(2,1)S(1)} %get-tuple-element.2), channel_id=1, source_target_pairs={{0,120},{8,112},{16,104},{24,96},{32,88},{40,80},{48,72},{56,64},{... | collective-permute-start | bytes 196616 | tf_op jit(solution)/shard_map/ppermute | solution.py:29
Sparse Core Ops, SparseCore 0:
  9.7 33.2 all-gather.2
  58.0 13.9 reduce-scatter.2
  75.0 72.3 all-gather.4
  200.1 34.0 reduce-scatter.4
